TPU v7x, 32 devices: a whole 2x2x4 slice. The times are simulated.
32 devices in a mesh: groups: 2 (over x), date: 8 (over z, y), row: 2 (over core).
Axes of the slice: x: 2, y: 2, z: 4, core: 2. Of those that a mesh axis runs over, the one named last changes fastest.
Arguments:
- scenes: bfloat16 [16, 4, 512, 1024], P(('groups', 'date'), None, 'row'), parts along dimension 0, may hold values from -6 to 6
- resample_taps: float32 [2, 4, 7], replicated, may hold values from 0 to 0.35
- clear_mask: int32 [16, 128, 8], P('groups', ('row', 'date')), parts along dimension 0, may hold values 0 or 1
Outputs:
- smooth_fine: bfloat16 [16, 4, 512, 1024], P('groups', None, ('row', 'date')), parts along dimension 0
- smooth_half: bfloat16 [16, 4, 256, 512], P('groups', None, ('row', 'date')), parts along dimension 0
- smooth_quarter: bfloat16 [16, 4, 128, 256], P('groups', None, ('row', 'date')), parts along dimension 0
There are 2 independent parts, one for each index of `groups`. A program takes and returns all parts, laid end to end along the dimension named above; an argument that names none is the same for every part. Nothing has to cross between parts.
Inputs may be any that keep to these rules, and one draw needn't show every extreme that they name: `clear_mask`: 1 marks a clear block, 0 a cloudy one.
All inputs are finite; a program needn't handle non-finite values.
Results may differ from a plain program's by a relative error of at most 0.005.
Values may be sent and summed in bfloat16 or wider, within the bound.
No kernel may reach another device: no remote copies, remote signals or barrier semaphores. Data moves between devices by JAX's collectives and lax.ppermute only.
A program may use at most 128 MiB of HBM per device.

v0:
```python
import math
import jax
import jax.numpy as jnp
from jax import lax
from jax.sharding import PartitionSpec as P

gap_weights = [math.exp(-((k - 4) ** 2) / 8.0) for k in range(9)]
savgol_coeffs = [c / 231.0 for c in [-21.0, 14.0, 39.0, 54.0, 59.0, 54.0, 39.0, 14.0, -21.0]]
pyramid_filter = [0.125, 0.375, 0.375, 0.125]


def padded(block, sides, width):
    for axis, dim in sides:
        count = lax.axis_size(axis)
        forward = [(i, i + 1) for i in range(count - 1)]
        backward = [(target, source) for source, target in forward]
        low = lax.ppermute(
            lax.slice_in_dim(block, block.shape[dim] - width, None, axis=dim), axis, forward
        )
        high = lax.ppermute(lax.slice_in_dim(block, 0, width, axis=dim), axis, backward)
        block = jnp.concatenate([low, block, high], axis=dim)
    return block


def valid_taps(values, taps, axis):
    count = values.shape[axis] - 6
    total = jnp.zeros(values.shape[:axis] + (count,) + values.shape[axis + 1 :], jnp.float32)
    for k in range(7):
        shape = [1] * values.ndim
        shape[-3] = taps.shape[0]
        total = total + taps[:, k].reshape(shape) * lax.slice_in_dim(values, k, k + count, 1, axis)
    return total


def column_resample(values, taps):
    width = values.shape[3]
    source = lax.broadcasted_iota(jnp.int32, (width, width), 0)
    target = lax.broadcasted_iota(jnp.int32, (width, width), 1)
    offset = source - target + 3
    table = jnp.zeros((taps.shape[0], width, width), jnp.float32)
    for k in range(7):
        table = table + taps[:, k][:, None, None] * (offset == k).astype(jnp.float32)[None]
    return jnp.einsum(
        "tbrc,bcd->tbrd", values.astype(jnp.float32), table, precision=lax.Precision.HIGHEST
    )


def halve_columns(values):
    width = values.shape[3]
    source = lax.broadcasted_iota(jnp.int32, (width, width // 2), 0)
    target = lax.broadcasted_iota(jnp.int32, (width, width // 2), 1)
    place = source - 2 * target + 1
    table = jnp.zeros((width, width // 2), jnp.float32)
    for p in range(4):
        table = table + pyramid_filter[p] * (place == p).astype(jnp.float32)
    return jnp.dot(values, table, precision=lax.Precision.HIGHEST)


def halve_rows(extended):
    pairs_count = extended.shape[2] // 2
    pairs = extended.reshape(extended.shape[:2] + (pairs_count, 2) + extended.shape[3:])
    even = pairs[:, :, :, 0]
    odd = pairs[:, :, :, 1]
    return (
        pyramid_filter[0] * even[:, :, :-1]
        + pyramid_filter[1] * odd[:, :, :-1]
        + pyramid_filter[2] * even[:, :, 1:]
        + pyramid_filter[3] * odd[:, :, 1:]
    )


def decimate_rim(extended):
    return halve_columns(halve_rows(extended))


def keep_rows(values, first, total):
    places = first + lax.iota(jnp.int32, values.shape[2])
    inside = (places >= 0) & (places < total)
    return jnp.where(inside[None, None, :, None], values, 0.0)


def smooth(level, clear):
    values = level.astype(jnp.float32)
    dates = values.shape[0]
    clear4 = clear[:, None]
    weight = 0.1 + 0.9 * clear4
    weighted = jnp.pad(weight * values, ((4, 4), (0, 0), (0, 0), (0, 0)))
    weight_pad = jnp.pad(weight, ((4, 4), (0, 0), (0, 0), (0, 0)))
    numer = jnp.zeros_like(values)
    denom = jnp.zeros_like(weight)
    for k in range(9):
        numer = numer + gap_weights[k] * weighted[k : k + dates]
        denom = denom + gap_weights[k] * weight_pad[k : k + dates]
    filled = clear4 * values + (1.0 - clear4) * (numer / denom)
    edged = jnp.pad(filled, ((4, 4), (0, 0), (0, 0), (0, 0)), mode="edge")
    result = jnp.zeros_like(values)
    for k in range(9):
        result = result + savgol_coeffs[k] * edged[k : k + dates]
    return result.astype(jnp.bfloat16)


def expand_mask(clear_mask, row_rep, col_rep):
    grown = jnp.repeat(jnp.repeat(clear_mask, row_rep, axis=1), col_rep, axis=2)
    return grown.astype(jnp.float32)


def local(scenes, resample_taps, clear_mask):
    rows = scenes.shape[2]
    extended = padded(scenes, (("row", 2),), 6)
    across = column_resample(extended, resample_taps[0])
    resampled_wide = valid_taps(across, resample_taps[1], 2)
    band_index = lax.axis_index("row")
    total_rows = rows * lax.axis_size("row")
    resampled_wide = keep_rows(resampled_wide, band_index * rows - 3, total_rows)
    half_wide = decimate_rim(resampled_wide)
    half_wide = keep_rows(half_wide, band_index * (rows // 2) - 1, total_rows // 2)
    resampled = resampled_wide[:, :, 3 : 3 + rows]
    half = half_wide[:, :, 1 : 1 + rows // 2]
    quarter = decimate_rim(half_wide)
    level_zero = resampled.astype(jnp.bfloat16)
    level_one = half.astype(jnp.bfloat16)
    level_two = quarter.astype(jnp.bfloat16)
    clear_fine = expand_mask(clear_mask, 4, 128)
    clear_half = expand_mask(clear_mask, 2, 64)
    clear_quarter = expand_mask(clear_mask, 1, 32)
    smooth_fine = smooth(
        lax.all_to_all(level_zero, "date", split_axis=2, concat_axis=0, tiled=True), clear_fine
    )
    smooth_half = smooth(
        lax.all_to_all(level_one, "date", split_axis=2, concat_axis=0, tiled=True), clear_half
    )
    smooth_quarter = smooth(
        lax.all_to_all(level_two, "date", split_axis=2, concat_axis=0, tiled=True), clear_quarter
    )
    return (smooth_fine, smooth_half, smooth_quarter)


def solution(mesh):
    in_specs = (P(("groups", "date"), None, "row", None), P(), P("groups", ("row", "date"), None))
    out_specs = (
        P("groups", None, ("row", "date"), None),
        P("groups", None, ("row", "date"), None),
        P("groups", None, ("row", "date"), None),
    )
    return jax.shard_map(local, mesh=mesh, in_specs=in_specs, out_specs=out_specs, check_vma=False)
```

profile of v0, /device:TPU:0, one launch (start us, length us, event | category | flops | bytes accessed | tf_op | source)
XLA Modules:
  0.0 176.9 jit_solution(12469758215546184341)
XLA Ops:
  0.6 0.9 fusion.313
  1.5 2.4 %collective-permute-start = (bf16[1,4,6,1024]{3,2,1,0:T(8,128)(2,1)S(1)}, bf16[1,4,6,1024]{3,2,1,0:T(8,128)(2,1)S(1)}, u32[]{:S(2)}, u32[]{:S(2)}) collective-permute-start(bf16[1,4,6,1024]{3,2,1,0:T(8,128)(2,1)S(1)} %get-tuple-element.21), channel_id=1, source_target_pairs={{0,1},{2,3},{4,5},{6,7},{8,9},{10,11},{12,13},{14,15},{16,17},{18,... | collective-permute-start | bytes 147464 | tf_op jit(solution)/shard_map/ppermute | solution.py:17
  3.9 1.3 collective-permute-start.1
  5.2 4.3 %fusion.83 = (f32[1024,1024]{1,0:T(8,128)}, f32[1024,1024]{1,0:T(8,128)}) fusion(), kind=kLoop, calls=%fused_computation.132 | loop fusion | flops 6291456 | bytes 8388608 | tf_op jit(solution)/shard_map/convert_element_type | solution.py:42
  9.5 4.3 %fusion.85 = (f32[1024,1024]{1,0:T(8,128)}, f32[1024,1024]{1,0:T(8,128)}) fusion(), kind=kLoop, calls=%fused_computation.134 | loop fusion | flops 6291456 | bytes 8388608 | tf_op jit(solution)/shard_map/convert_element_type | solution.py:42
  13.8 4.3 %fusion.87 = (f32[1024,1024]{1,0:T(8,128)}, f32[1024,1024]{1,0:T(8,128)}) fusion(), kind=kLoop, calls=%fused_computation.136 | loop fusion | flops 6291456 | bytes 8388608 | tf_op jit(solution)/shard_map/convert_element_type | solution.py:42
  18.2 2.5 %fusion.89 = f32[1024,1024]{1,0:T(8,128)} fusion(), kind=kLoop, calls=%fused_computation.138 | loop fusion | flops 4194304 | bytes 4194304 | tf_op jit(solution)/shard_map/convert_element_type | solution.py:42
  20.7 0.4 slice_reduce_fusion.12
  21.1 0.0 collective-permute-done
  21.1 23.9 %fusion.96 = f32[1,4,268,1024]{3,2,1,0:T(8,128)S(1)} fusion(bf16[1,4,6,1024]{3,2,1,0:T(8,128)(2,1)S(1)} %collective-permute-done.1, bf16[1,4,256,1024]{3,2,1,0:T(8,128)(2,1)S(1)} %copy-done.1, bf16[1,4,6,1024]{3,2,1,0:T(8,128)(2,1)S(1)} %collective-permute-done, f32[1024,1024]{1,0:T(8,128)} %fusion.89, f32[4]{0:T(128)S(1)} %get-tuple-element.11, ...), kind=kOutput, calls=%fused_computation.152 | convolution fusion | flops 13549993984 | bytes 35946608 | tf_op jit(solution)/shard_map/tbrc,bcd->tbrd/dot_general | solution.py:43
  45.1 3.8 %fusion.29 = f32[1,4,262,1024]{3,2,1,0:T(8,128)S(1)} fusion(f32[1,4,268,1024]{3,2,1,0:T(8,128)S(1)} %fusion.96, f32[4]{0:T(128)S(1)} %get-tuple-element.42, f32[4]{0:T(128)S(1)} %get-tuple-element.41, f32[4]{0:T(128)S(1)} %get-tuple-element.40, f32[4]{0:T(128)S(1)} %get-tuple-element.39, f32[4]{0:T(128)S(1)} %get-tuple-element.38, ...), kind=kLoop, calls=%fused_computation.66 | loop fusion | flops 15024128 | bytes 34341240 | tf_op jit(solution)/shard_map/jit(_where)/select_n | solution.py:79
  48.9 2.8 %copy.24 = f32[1,4,262,1024]{3,1,2,0:T(4,128)S(1)} copy(f32[1,4,262,1024]{3,2,1,0:T(8,128)S(1)} %fusion.29) | data formatting | bytes 8585216 | tf_op jit(solution)/shard_map/jit(_where)/select_n | solution.py:79
  51.7 1.0 slice_bitcast_fusion.1
  52.7 2.3 %fusion.100 = f32[4,130,1024]{2,0,1:T(4,128)S(1)} fusion(f32[1,4,131,1024]{3,1,2,0:T(4,128)S(1)} %get-tuple-element.18, f32[1,4,131,1024]{3,1,2,0:T(4,128)S(1)} %get-tuple-element.17), kind=kLoop, calls=%fused_computation.157 | loop fusion | flops 3727360 | bytes 10649600 | tf_op jit(solution)/shard_map/reshape.35
  55.0 5.7 %fusion.119 = f32[4,130,512]{2,1,0:T(8,128)S(1)} fusion(f32[4,130,1024]{2,0,1:T(4,128)S(1)} %fusion.100, s32[512]{0:T(512)S(1)} %iota_multiply_fusion, pred[130]{0:T(512)(128)(4,1)S(1)} %compare_and_fusion), kind=kOutput, calls=%fused_computation.182 | convolution fusion | flops 3278639104 | bytes 3197058 | tf_op jit(solution)/shard_map/dot_general | solution.py:56
  60.7 0.7 copy.29
  61.4 0.2 slice_bitcast_fusion.3
  61.6 0.3 fusion.192
  61.9 0.0 copy-start.4
  61.9 0.9 fusion.124
  62.7 0.8 copy.32
  63.5 6.7 %all-to-all-start.2 = ((bf16[1,4,64,256]{3,1,0,2:T(4,128)(2,1)}), bf16[1,4,64,256]{3,1,0,2:T(4,128)(2,1)S(1)}, u32[]{:S(2)}, u32[]{:S(2)}) async-start(bf16[1,4,64,256]{3,1,0,2:T(4,128)(2,1)} %copy.32), calls=%async_computation.2 | async-start | bytes 262144 | tf_op jit(solution)/shard_map/all_to_all | solution.py:133
  70.2 0.1 convert_bitcast_fusion
  70.3 0.1 slice.555
  70.4 1.2 copy.27
  71.6 6.8 %all-to-all-done.2 = bf16[1,4,64,256]{3,1,0,2:T(4,128)(2,1)S(1)} async-done(((bf16[1,4,64,256]{3,1,0,2:T(4,128)(2,1)}), bf16[1,4,64,256]{3,1,0,2:T(4,128)(2,1)S(1)}, u32[]{:S(2)}, u32[]{:S(2)}) %all-to-all-start.2) | async-done | bytes 131104 | tf_op jit(solution)/shard_map/all_to_all | solution.py:133
  78.4 3.5 %all-to-all-start.1 = ((bf16[1,4,128,512]{3,1,0,2:T(4,128)(2,1)}), bf16[1,4,128,512]{3,1,0,2:T(4,128)(2,1)S(1)}, u32[]{:S(2)}, u32[]{:S(2)}) async-start(bf16[1,4,128,512]{3,1,0,2:T(4,128)(2,1)} %copy.27), calls=%async_computation.1 | async-start | bytes 1048576 | tf_op jit(solution)/shard_map/all_to_all | solution.py:130
  81.9 0.1 broadcast_in_dim.86
  82.1 0.1 add.544
  82.2 2.8 %slice.1298 = bf16[1,4,256,1024]{3,2,1,0:T(8,128)(2,1)S(1)} slice(f32[1,4,262,1024]{3,2,1,0:T(8,128)} %copy-done), slice={[0:1], [0:4], [3:259], [0:1024]} | slice | bytes 4194304 | tf_op jit(solution)/shard_map/slice | solution.py:117
  85.0 2.9 %copy.22 = bf16[1,4,256,1024]{3,1,0,2:T(4,128)(2,1)} copy(bf16[1,4,256,1024]{3,2,1,0:T(8,128)(2,1)S(1)} %slice.1298) | data formatting | bytes 4194304 | tf_op jit(solution)/shard_map/slice | solution.py:117
  88.0 8.6 %all-to-all-done.1 = bf16[1,4,128,512]{3,1,0,2:T(4,128)(2,1)S(1)} async-done(((bf16[1,4,128,512]{3,1,0,2:T(4,128)(2,1)}), bf16[1,4,128,512]{3,1,0,2:T(4,128)(2,1)S(1)}, u32[]{:S(2)}, u32[]{:S(2)}) %all-to-all-start.1) | async-done | bytes 524320 | tf_op jit(solution)/shard_map/all_to_all | solution.py:130
  96.6 4.6 %all-to-all-start = ((bf16[1,4,256,1024]{3,1,0,2:T(4,128)(2,1)}), bf16[1,4,256,1024]{3,1,0,2:T(4,128)(2,1)}, u32[]{:S(2)}, u32[]{:S(2)}) async-start(bf16[1,4,256,1024]{3,1,0,2:T(4,128)(2,1)} %copy.22), calls=%async_computation | async-start | bytes 4194304 | tf_op jit(solution)/shard_map/all_to_all | solution.py:127
  101.2 0.1 broadcast_in_dim.85
  101.4 0.1 convert_element_type.222
  101.5 0.2 broadcast_in_dim.80
  101.7 0.1 convert_element_type.216
  101.9 0.2 broadcast_in_dim.84
  102.1 0.1 add.509
  102.3 0.3 broadcast_in_dim.74
  102.6 0.2 convert_element_type.202
  102.8 1.3 broadcast_in_dim.78
  104.2 1.4 add.471
  105.6 0.1 fusion.242
  105.7 0.1 broadcast_subtract_fusion.1
  105.8 1.4 fusion.155
  107.1 1.2 broadcast_subtract_fusion
  108.3 0.1 bitcast_multiply_fusion.4
  108.4 0.1 fusion.269
  108.6 0.8 fusion.216
  109.4 0.1 convert.19
  109.6 0.3 bitcast_multiply_fusion.2
  109.9 0.7 fusion.182
  110.6 0.1 reshape.283
  110.7 0.1 reshape.284
  110.7 2.0 %fusion.129 = bf16[8,4,16,512]{3,2,1,0:T(8,128)(2,1)} fusion(f32[8,4,16,512]{3,2,1,0:T(8,128)S(1)} %fusion.182, f32[4,4,16,512]{3,2,1,0:T(8,128)S(1)} %reshape.284, f32[4,4,16,512]{3,2,1,0:T(8,128)S(1)} %reshape.283), kind=kLoop, calls=%fused_computation.205 | loop fusion | flops 6815744 | bytes 2621440 | tf_op jit(solution)/shard_map/convert_element_type | solution.py:99
  112.7 36.2 %all-to-all-done = bf16[1,4,256,1024]{3,1,0,2:T(4,128)(2,1)} async-done(((bf16[1,4,256,1024]{3,1,0,2:T(4,128)(2,1)}), bf16[1,4,256,1024]{3,1,0,2:T(4,128)(2,1)}, u32[]{:S(2)}, u32[]{:S(2)}) %all-to-all-start) | async-done | bytes 2097184 | tf_op jit(solution)/shard_map/all_to_all | solution.py:127
  149.0 2.8 %convert.18 = f32[1,4,8,32,1024]{4,1,3,2,0:T(4,128)S(1)} convert(bf16[1,4,8,32,1024]{4,1,3,2,0:T(4,128)(2,1)} %bitcast.43) | non-fusion elementwise | flops 1048576 | bytes 6291456 | tf_op jit(solution)/shard_map/convert_element_type | solution.py:83
  151.8 4.5 %bitcast_multiply_fusion = f32[8,4,32,1024]{3,2,1,0:T(8,128)} fusion(f32[1,4,8,32,1024]{4,1,3,2,0:T(4,128)S(1)} %convert.18, f32[8,32,1024]{2,1,0:T(8,128)S(1)} %get-tuple-element.28), kind=kLoop, calls=%fused_computation.121 | loop fusion | flops 1048576 | bytes 9437184 | tf_op jit(solution)/shard_map/mul | solution.py:87
  156.4 13.9 %fusion.75 = f32[8,4,32,1024]{3,2,1,0:T(8,128)S(1)} fusion(f32[8,4,32,1024]{3,2,1,0:T(8,128)} %bitcast_multiply_fusion, f32[1,4,8,32,1024]{4,1,3,2,0:T(4,128)S(1)} %convert.18, f32[8,32,1024]{2,1,0:T(8,128)} %fusion.155, f32[8,32,1024]{2,1,0:T(8,128)} %get-tuple-element.27, f32[8,32,1024]{2,1,0:T(8,128)S(1)} %convert_element_type.202), kind=kLoop, calls=%fused_computation.123 | loop fusion | flops 20971520 | bytes 15728640 | tf_op jit(solution)/shard_map/add | solution.py:94
  170.3 0.1 slice_bitcast_fusion.5
  170.4 0.2 reshape.279
  170.6 0.3 reshape.280
  170.9 5.8 %fusion.39 = bf16[8,4,32,1024]{3,2,1,0:T(8,128)(2,1)} fusion(f32[8,4,32,1024]{3,2,1,0:T(8,128)S(1)} %fusion.75, f32[4,4,32,1024]{3,2,1,0:T(8,128)S(1)} %reshape.280, f32[4,4,32,1024]{3,2,1,0:T(8,128)S(1)} %reshape.279), kind=kLoop, calls=%fused_computation.82 | loop fusion | flops 27262976 | bytes 10485760 | tf_op jit(solution)/shard_map/convert_element_type | solution.py:99
  (30 shorter events, 0.3 us)
Async XLA Ops:
  1.5 19.6 %collective-permute-start = (bf16[1,4,6,1024]{3,2,1,0:T(8,128)(2,1)S(1)}, bf16[1,4,6,1024]{3,2,1,0:T(8,128)(2,1)S(1)}, u32[]{:S(2)}, u32[]{:S(2)}) collective-permute-start(bf16[1,4,6,1024]{3,2,1,0:T(8,128)(2,1)S(1)} %get-tuple-element.21), channel_id=1, source_target_pairs={{0,1},{2,3},{4,5},{6,7},{8,9},{10,11},{12,13},{14,15},{16,17},{18,... | collective-permute-start | bytes 147464 | tf_op jit(solution)/shard_map/ppermute | solution.py:17
  3.9 17.2 %collective-permute-start.1 = (bf16[1,4,6,1024]{3,2,1,0:T(8,128)(2,1)S(1)}, bf16[1,4,6,1024]{3,2,1,0:T(8,128)(2,1)S(1)}, u32[]{:S(2)}, u32[]{:S(2)}) collective-permute-start(bf16[1,4,6,1024]{3,2,1,0:T(8,128)(2,1)S(1)} %get-tuple-element.22), channel_id=1, source_target_pairs={{1,0},{3,2},{5,4},{7,6},{9,8},{11,10},{13,12},{15,14},{17,16},{19,... | collective-permute-start | bytes 147464 | tf_op jit(solution)/shard_map/ppermute | solution.py:20
  18.2 2.5 %copy-start.5 = (f32[2,4,7]{2,1,0:T(4,128)S(1)}, f32[2,4,7]{2,1,0:T(4,128)}, u32[]{:S(2)}) copy-start(f32[2,4,7]{2,1,0:T(4,128)} %param.4) | copy-start | bytes 676
  18.2 2.9 %copy-start.1 = (bf16[1,4,256,1024]{3,2,1,0:T(8,128)(2,1)S(1)}, bf16[1,4,256,1024]{3,2,1,0:T(8,128)(2,1)}, u32[]{:S(2)}) copy-start(bf16[1,4,256,1024]{3,2,1,0:T(8,128)(2,1)} %param.3) | copy-start | bytes 6291460
  48.9 2.8 %copy-start = (f32[1,4,262,1024]{3,2,1,0:T(8,128)}, f32[1,4,262,1024]{3,2,1,0:T(8,128)S(1)}, u32[]{:S(2)}) copy-start(f32[1,4,262,1024]{3,2,1,0:T(8,128)S(1)} %fusion.29) | copy-start | bytes 12877828
  61.9 20.0 %copy-start.4 = (s32[8,8,8]{2,1,0:T(8,128)S(1)}, s32[8,8,8]{2,1,0:T(8,128)}, u32[]{:S(2)}) copy-start(s32[8,8,8]{2,1,0:T(8,128)} %param.5) | copy-start | bytes 6148
  63.5 14.9 %all-to-all-start.2 = ((bf16[1,4,64,256]{3,1,0,2:T(4,128)(2,1)}), bf16[1,4,64,256]{3,1,0,2:T(4,128)(2,1)S(1)}, u32[]{:S(2)}, u32[]{:S(2)}) async-start(bf16[1,4,64,256]{3,1,0,2:T(4,128)(2,1)} %copy.32), calls=%async_computation.2 | async-start | bytes 262144 | tf_op jit(solution)/shard_map/all_to_all | solution.py:133
  78.4 9.6 %copy-start.2 = (bf16[1,4,64,256]{3,1,0,2:T(4,128)(2,1)}, bf16[1,4,64,256]{3,1,0,2:T(4,128)(2,1)S(1)}, u32[]{:S(2)}) copy-start(bf16[1,4,64,256]{3,1,0,2:T(4,128)(2,1)S(1)} %all-to-all-done.2) | copy-start | bytes 393220
  78.4 18.2 %all-to-all-start.1 = ((bf16[1,4,128,512]{3,1,0,2:T(4,128)(2,1)}), bf16[1,4,128,512]{3,1,0,2:T(4,128)(2,1)S(1)}, u32[]{:S(2)}, u32[]{:S(2)}) async-start(bf16[1,4,128,512]{3,1,0,2:T(4,128)(2,1)} %copy.27), calls=%async_computation.1 | async-start | bytes 1048576 | tf_op jit(solution)/shard_map/all_to_all | solution.py:130
  96.6 52.4 %all-to-all-start = ((bf16[1,4,256,1024]{3,1,0,2:T(4,128)(2,1)}), bf16[1,4,256,1024]{3,1,0,2:T(4,128)(2,1)}, u32[]{:S(2)}, u32[]{:S(2)}) async-start(bf16[1,4,256,1024]{3,1,0,2:T(4,128)(2,1)} %copy.22), calls=%async_computation | async-start | bytes 4194304 | tf_op jit(solution)/shard_map/all_to_all | solution.py:127
  104.2 4.2 %copy-start.3 = (bf16[1,4,64,256]{3,1,0,2:T(4,128)(2,1)S(1)}, bf16[1,4,64,256]{3,1,0,2:T(4,128)(2,1)}, u32[]{:S(2)}) copy-start(bf16[1,4,64,256]{3,1,0,2:T(4,128)(2,1)} %copy-done.2) | copy-start | bytes 393220
where the time goes:
time: 180 us; the launch traced here: 177 us
  other arithmetic  56 us (31%)
  waiting for transfers between devices  51.7 us (29%)
  matrix products  30.5 us (17%)
  local copies, waits for them, and re-layouts  19 us (11%)
  starting transfers between devices  18.4 us (10%)
    all_to_all x1, waiting for transfers between devices, local(): lax.all_to_all(level_zero, 'date', split_axis=2, concat_axis=0, tiled=True)  36.2 us
    dot_general x1, matrix products, column_resample(): jnp.einsum('tbrc,bcd->tbrd', values.astype(jnp.float32), table, precision...  23.9 us
    convert_element_type x4, other arithmetic, column_resample(): (offset == k).astype(jnp.float32)[None]  15.4 us
    add x3, other arithmetic, smooth(): filled = clear4 * values + (1.0 - clear4) * (numer / denom)  14.7 us
    convert_element_type x3, other arithmetic, smooth(): return result.astype(jnp.bfloat16)  8.65 us
    all_to_all x1, waiting for transfers between devices, local(): lax.all_to_all(level_one, 'date', split_axis=2, concat_axis=0, tiled=True)  8.64 us
    all_to_all x1, waiting for transfers between devices, local(): lax.all_to_all(level_two, 'date', split_axis=2, concat_axis=0, tiled=True)  6.81 us
    all_to_all x1, starting transfers between devices, local(): lax.all_to_all(level_two, 'date', split_axis=2, concat_axis=0, tiled=True)  6.67 us
  transfers between devices with their start and end apart: 5, of which 3 were waited for; matrix products, arithmetic and copies ran while one was open for 20% of the time, Pallas kernels for 0%

commit v1 on v0

--- a/solution.py
+++ b/solution.py
@@ -124,7 +124,13 @@
     clear_half = expand_mask(clear_mask, 2, 64)
     clear_quarter = expand_mask(clear_mask, 1, 32)
     smooth_fine = smooth(
-        lax.all_to_all(level_zero, "date", split_axis=2, concat_axis=0, tiled=True), clear_fine
+        jnp.concatenate(
+            lax.all_to_all(
+                jnp.stack(jnp.split(level_zero, lax.axis_size("date"), axis=2)), "date", 0, 0
+            ),
+            axis=0,
+        ),
+        clear_fine,
     )
     smooth_half = smooth(
         lax.all_to_all(level_one, "date", split_axis=2, concat_axis=0, tiled=True), clear_half

time: 180 us -> 163 us (0.906); the launches traced: 177 us -> 162 us
  waiting for transfers between devices: 51.7 us -> 37 us
  local copies, waits for them, and re-layouts: 19 us -> 27.2 us
  other arithmetic: 56 us -> 49.4 us
    all_to_all x1, waiting for transfers between devices: 36.2 us -> 21.6 us  [local(): lax.all_to_all(jnp.stack(jnp.split(level_zero, lax.axis_size('date'), axi...]
    add x3, other arithmetic: 14.7 us -> 6 us  [smooth(): filled = clear4 * values + (1.0 - clear4) * (numer / denom)]
    div x3, other arithmetic: 1.48 us -> 8.49 us  [smooth(): filled = clear4 * values + (1.0 - clear4) * (numer / denom)]
    slice x2 -> x0, local copies, waits for them, and re-layouts: 5.77 us -> none  [local(): resampled = resampled_wide[:, :, 3:3 + rows]]
    unnamed x12 -> x25, local copies, waits for them, and re-layouts: 0.03 us -> 5.45 us
    another operation x2 -> x3, other arithmetic: 2.58 us -> 6.55 us
    select_n x2 -> x1, other arithmetic: 3.91 us -> 0.07 us  [keep_rows(): return jnp.where(inside[None, None, :, None], values, 0.0)]
    all_to_all x1, waiting for transfers between devices: 6.81 us -> 3.79 us  [local(): lax.all_to_all(level_two, 'date', split_axis=2, concat_axis=0, tiled=True)]
  transfers between devices with their start and end apart: 5 -> 5, of which waited for: 3 -> 3; matrix products, arithmetic and copies ran while one was open for 20% -> 31% of each run, Pallas kernels for 0% -> 0%
where the time goes in v1:
time: 163 us; the launch traced here: 162 us
  other arithmetic  49.4 us (30%)
  waiting for transfers between devices  37 us (23%)
  matrix products  30.2 us (19%)
  local copies, waits for them, and re-layouts  27.2 us (17%)
  starting transfers between devices  17.7 us (11%)
    dot_general x1, matrix products, column_resample(): jnp.einsum('tbrc,bcd->tbrd', values.astype(jnp.float32), table, precision...  23.6 us
    all_to_all x1, waiting for transfers between devices, local(): lax.all_to_all(jnp.stack(jnp.split(level_zero, lax.axis_size('date'), axi...  21.6 us
    convert_element_type x4, other arithmetic, column_resample(): (offset == k).astype(jnp.float32)[None]  15.4 us
    all_to_all x1, waiting for transfers between devices, local(): lax.all_to_all(level_one, 'date', split_axis=2, concat_axis=0, tiled=True)  11.6 us
    convert_element_type x3, other arithmetic, smooth(): return result.astype(jnp.bfloat16)  8.5 us
    div x3, other arithmetic, smooth(): filled = clear4 * values + (1.0 - clear4) * (numer / denom)  8.49 us
    all_to_all x1, starting transfers between devices, local(): lax.all_to_all(level_two, 'date', split_axis=2, concat_axis=0, tiled=True)  6.66 us
    dot_general x2, matrix products, halve_columns(): return jnp.dot(values, table, precision=lax.Precision.HIGHEST)  6.56 us
  transfers between devices with their start and end apart: 5, of which 3 were waited for; matrix products, arithmetic and copies ran while one was open for 31% of the time, Pallas kernels for 0%

profile of v1, /device:TPU:0, one launch (start us, length us, event | category | flops | bytes accessed | tf_op | source)
XLA Modules:
  0.0 162.5 jit_solution(9615387475312363810)
XLA Ops:
  0.6 0.9 fusion.323
  1.5 2.4 %collective-permute-start = (bf16[1,4,6,1024]{3,2,1,0:T(8,128)(2,1)S(1)}, bf16[1,4,6,1024]{3,2,1,0:T(8,128)(2,1)S(1)}, u32[]{:S(2)}, u32[]{:S(2)}) collective-permute-start(bf16[1,4,6,1024]{3,2,1,0:T(8,128)(2,1)S(1)} %get-tuple-element.23), channel_id=1, source_target_pairs={{0,1},{2,3},{4,5},{6,7},{8,9},{10,11},{12,13},{14,15},{16,17},{18,... | collective-permute-start | bytes 147464 | tf_op jit(solution)/shard_map/ppermute | solution.py:17
  3.9 1.3 collective-permute-start.1
  5.2 4.3 %fusion.83 = (f32[1024,1024]{1,0:T(8,128)}, f32[1024,1024]{1,0:T(8,128)}) fusion(), kind=kLoop, calls=%fused_computation.131 | loop fusion | flops 6291456 | bytes 8388608 | tf_op jit(solution)/shard_map/convert_element_type | solution.py:42
  9.5 4.3 %fusion.85 = (f32[1024,1024]{1,0:T(8,128)}, f32[1024,1024]{1,0:T(8,128)}) fusion(), kind=kLoop, calls=%fused_computation.133 | loop fusion | flops 6291456 | bytes 8388608 | tf_op jit(solution)/shard_map/convert_element_type | solution.py:42
  13.8 4.3 %fusion.87 = (f32[1024,1024]{1,0:T(8,128)}, f32[1024,1024]{1,0:T(8,128)}) fusion(), kind=kLoop, calls=%fused_computation.135 | loop fusion | flops 6291456 | bytes 8388608 | tf_op jit(solution)/shard_map/convert_element_type | solution.py:42
  18.2 2.5 %fusion.89 = f32[1024,1024]{1,0:T(8,128)} fusion(), kind=kLoop, calls=%fused_computation.137 | loop fusion | flops 4194304 | bytes 4194304 | tf_op jit(solution)/shard_map/convert_element_type | solution.py:42
  20.7 0.4 slice_reduce_fusion.12
  21.1 0.1 broadcast_in_dim.86
  21.2 0.1 add.544
  21.4 23.6 %fusion.96 = f32[1,4,268,1024]{3,2,1,0:T(8,128)S(1)} fusion(bf16[1,4,6,1024]{3,2,1,0:T(8,128)(2,1)S(1)} %collective-permute-done.1, bf16[1,4,256,1024]{3,2,1,0:T(8,128)(2,1)S(1)} %copy-done.1, bf16[1,4,6,1024]{3,2,1,0:T(8,128)(2,1)S(1)} %collective-permute-done, f32[1024,1024]{1,0:T(8,128)} %fusion.89, f32[4]{0:T(128)S(1)} %get-tuple-element.11, ...), kind=kOutput, calls=%fused_computation.151 | convolution fusion | flops 13549993984 | bytes 35946608 | tf_op jit(solution)/shard_map/tbrc,bcd->tbrd/dot_general | solution.py:43
  45.1 3.9 %fusion.321 = (bf16[1,4,262,1024]{3,2,1,0:T(8,128)(2,1)S(1)}, f32[1,4,262,1024]{3,2,1,0:T(8,128)S(1)}) fusion(f32[1,4,268,1024]{3,2,1,0:T(8,128)S(1)} %fusion.96, f32[4]{0:T(128)S(1)} %get-tuple-element.44, f32[4]{0:T(128)S(1)} %get-tuple-element.43, f32[4]{0:T(128)S(1)} %get-tuple-element.42, f32[4]{0:T(128)S(1)} %get-tuple-element.41, ...), kind=kLoop, calls=%fused_computation.469 | loop fusion | flops 16097280 | bytes 36487544 | tf_op jit(solution)/shard_map/convert.9
  49.0 2.8 %copy.20 = f32[1,4,262,1024]{3,1,2,0:T(4,128)S(1)} copy(f32[1,4,262,1024]{3,2,1,0:T(8,128)S(1)} %get-tuple-element.18) | data formatting | bytes 8585216 | tf_op jit(solution)/shard_map/jit(_where)/select_n | solution.py:79
  51.7 1.0 slice_bitcast_fusion.1
  52.7 2.3 %fusion.100 = f32[4,130,1024]{2,0,1:T(4,128)S(1)} fusion(f32[1,4,131,1024]{3,1,2,0:T(4,128)S(1)} %get-tuple-element.20, f32[1,4,131,1024]{3,1,2,0:T(4,128)S(1)} %get-tuple-element.19), kind=kLoop, calls=%fused_computation.156 | loop fusion | flops 3727360 | bytes 10649600 | tf_op jit(solution)/shard_map/reshape.36
  55.1 5.7 %fusion.119 = f32[4,130,512]{2,1,0:T(8,128)S(1)} fusion(f32[4,130,1024]{2,0,1:T(4,128)S(1)} %fusion.100, s32[512]{0:T(512)S(1)} %iota_multiply_fusion, pred[130]{0:T(512)(128)(4,1)S(1)} %compare_and_fusion), kind=kOutput, calls=%fused_computation.181 | convolution fusion | flops 3278639104 | bytes 3197058 | tf_op jit(solution)/shard_map/dot_general | solution.py:56
  60.8 0.7 copy.25
  61.5 0.1 convert_bitcast_fusion
  61.6 0.2 slice_bitcast_fusion.3
  61.7 0.3 fusion.192
  62.0 0.9 fusion.124
  62.9 0.8 copy.28
  63.7 6.7 %all-to-all-start.2 = ((bf16[1,4,64,256]{3,1,0,2:T(4,128)(2,1)}), bf16[1,4,64,256]{3,1,0,2:T(4,128)(2,1)S(1)}, u32[]{:S(2)}, u32[]{:S(2)}) async-start(bf16[1,4,64,256]{3,1,0,2:T(4,128)(2,1)} %copy.28), calls=%async_computation.2 | async-start | bytes 262144 | tf_op jit(solution)/shard_map/all_to_all | solution.py:139
  70.3 0.1 slice.559
  70.5 1.2 copy.23
  71.7 0.8 fusion.276
  72.4 0.8 fusion.275
  73.2 0.8 fusion.274
  74.0 0.8 fusion.273
  74.8 3.8 %all-to-all-done.2 = bf16[1,4,64,256]{3,1,0,2:T(4,128)(2,1)S(1)} async-done(((bf16[1,4,64,256]{3,1,0,2:T(4,128)(2,1)}), bf16[1,4,64,256]{3,1,0,2:T(4,128)(2,1)S(1)}, u32[]{:S(2)}, u32[]{:S(2)}) %all-to-all-start.2) | async-done | bytes 131104 | tf_op jit(solution)/shard_map/all_to_all | solution.py:139
  78.6 3.5 %all-to-all-start.1 = ((bf16[1,4,128,512]{3,1,0,2:T(4,128)(2,1)}), bf16[1,4,128,512]{3,1,0,2:T(4,128)(2,1)S(1)}, u32[]{:S(2)}, u32[]{:S(2)}) async-start(bf16[1,4,128,512]{3,1,0,2:T(4,128)(2,1)} %copy.23), calls=%async_computation.1 | async-start | bytes 1048576 | tf_op jit(solution)/shard_map/all_to_all | solution.py:136
  82.1 0.8 fusion.272
  82.8 0.8 fusion.271
  83.6 0.8 fusion.270
  84.4 0.8 fusion.269
  85.2 11.6 %all-to-all-done.1 = bf16[1,4,128,512]{3,1,0,2:T(4,128)(2,1)S(1)} async-done(((bf16[1,4,128,512]{3,1,0,2:T(4,128)(2,1)}), bf16[1,4,128,512]{3,1,0,2:T(4,128)(2,1)S(1)}, u32[]{:S(2)}, u32[]{:S(2)}) %all-to-all-start.1) | async-done | bytes 524320 | tf_op jit(solution)/shard_map/all_to_all | solution.py:136
  96.8 3.9 %all-to-all-start = ((bf16[8,1,4,32,1024]{4,3,2,1,0:T(8,128)(2,1)}), bf16[8,1,4,32,1024]{4,3,2,1,0:T(8,128)(2,1)S(1)}, u32[]{:S(2)}, u32[]{:S(2)}) async-start(bf16[8,1,4,32,1024]{4,3,2,1,0:T(8,128)(2,1)} %fusion.269), calls=%async_computation | async-start | bytes 4194304 | tf_op jit(solution)/shard_map/all_to_all | solution.py:128
  100.7 0.6 fusion.295
  101.3 0.1 broadcast_in_dim.85
  101.4 0.1 convert_element_type.214
  101.6 1.0 broadcast_in_dim.80
  102.6 1.2 convert_element_type.208
  103.8 1.0 broadcast_in_dim.84
  104.8 1.9 %add.509 = f32[8,1,16,512]{3,2,0,1:T(8,128)} reshape(f32[8,16,8,64]{3,2,1,0:T(8,128)} %broadcast_in_dim.84) | data formatting | bytes 524288 | tf_op jit(solution)/shard_map/add | solution.py:86
  106.8 1.3 broadcast_in_dim.74
  108.1 1.4 convert_element_type.196
  109.5 1.3 broadcast_in_dim.78
  110.9 2.4 %add.471 = f32[8,1,32,1024]{3,2,0,1:T(8,128)} reshape(f32[8,32,8,128]{3,2,1,0:T(8,128)} %broadcast_in_dim.78) | data formatting | bytes 2097152 | tf_op jit(solution)/shard_map/add | solution.py:86
  113.3 1.9 %fusion.242 = f32[8,16,512]{2,1,0:T(8,128)S(1)} fusion(f32[8,1,16,512]{3,2,0,1:T(8,128)} %add.509), kind=kLoop, calls=%fused_computation.349 | loop fusion | flops 1048576 | bytes 524288 | tf_op jit(solution)/shard_map/div | solution.py:94
  115.3 5.9 %fusion.155 = f32[8,32,1024]{2,1,0:T(8,128)} fusion(f32[8,1,32,1024]{3,2,0,1:T(8,128)} %add.471), kind=kLoop, calls=%fused_computation.230 | loop fusion | flops 4194304 | bytes 2097152 | tf_op jit(solution)/shard_map/div | solution.py:94
  121.2 1.6 %broadcast_subtract_fusion = (f32[8,32,1024]{2,1,0:T(8,128)}, f32[8,32,1024]{2,1,0:T(8,128)}) fusion(f32[8,32,1024]{2,1,0:T(8,128)S(1)} %convert_element_type.196), kind=kLoop, calls=%fused_computation.304 | loop fusion | flops 786432 | bytes 3145728 | tf_op jit(solution)/shard_map/sub | solution.py:94
  123.0 0.1 fusion.277
  123.2 0.8 fusion.216
  124.0 0.1 convert.17
  124.1 0.3 bitcast_multiply_fusion
  124.5 0.7 fusion.182
  125.3 2.0 %fusion.129 = bf16[8,4,16,512]{3,2,1,0:T(8,128)(2,1)} fusion(f32[8,4,16,512]{3,2,1,0:T(8,128)S(1)} %fusion.182, f32[4,4,16,512]{3,2,1,0:T(8,128)S(1)} %reshape.283, f32[4,4,16,512]{3,2,1,0:T(8,128)S(1)} %reshape.282), kind=kLoop, calls=%fused_computation.204 | loop fusion | flops 6815744 | bytes 2621440 | tf_op jit(solution)/shard_map/convert_element_type | solution.py:99
  127.3 21.6 %all-to-all-done = bf16[8,1,4,32,1024]{4,3,2,1,0:T(8,128)(2,1)S(1)} async-done(((bf16[8,1,4,32,1024]{4,3,2,1,0:T(8,128)(2,1)}), bf16[8,1,4,32,1024]{4,3,2,1,0:T(8,128)(2,1)S(1)}, u32[]{:S(2)}, u32[]{:S(2)}) %all-to-all-start) | async-done | bytes 2097184 | tf_op jit(solution)/shard_map/all_to_all | solution.py:128
  148.9 2.0 %convert_multiply_fusion = f32[8,4,32,1024]{3,2,1,0:T(8,128)S(1)} fusion(bf16[8,1,4,32,1024]{4,3,2,1,0:T(8,128)(2,1)S(1)} %all-to-all-done, f32[8,32,1024]{2,1,0:T(8,128)} %get-tuple-element.30), kind=kLoop, calls=%fused_computation.48 | loop fusion | flops 2097152 | bytes 7340032 | tf_op jit(solution)/shard_map/mul | solution.py:87
  150.9 5.2 %fusion.35 = f32[8,4,32,1024]{3,2,1,0:T(8,128)S(1)} fusion(f32[8,4,32,1024]{3,2,1,0:T(8,128)S(1)} %convert_multiply_fusion, bf16[8,1,4,32,1024]{4,3,2,1,0:T(8,128)(2,1)S(1)} %all-to-all-done, f32[8,32,1024]{2,1,0:T(8,128)} %fusion.155, f32[8,32,1024]{2,1,0:T(8,128)S(1)} %copy-done, f32[8,32,1024]{2,1,0:T(8,128)S(1)} %convert_element_type.196), kind=kLoop, calls=%fused_computation.80 | loop fusion | flops 22020096 | bytes 13631488 | tf_op jit(solution)/shard_map/add | solution.py:94
  156.1 0.1 slice_bitcast_fusion.5
  156.2 0.3 reshape.278
  156.5 0.3 reshape.279
  156.8 5.7 %fusion.40 = bf16[8,4,32,1024]{3,2,1,0:T(8,128)(2,1)} fusion(f32[8,4,32,1024]{3,2,1,0:T(8,128)S(1)} %fusion.35, f32[4,4,32,1024]{3,2,1,0:T(8,128)S(1)} %reshape.279, f32[4,4,32,1024]{3,2,1,0:T(8,128)S(1)} %reshape.278), kind=kLoop, calls=%fused_computation.85 | loop fusion | flops 27262976 | bytes 10485760 | tf_op jit(solution)/shard_map/convert_element_type | solution.py:99
  (41 shorter events, 0.5 us)
Async XLA Ops:
  1.5 19.8 %collective-permute-start = (bf16[1,4,6,1024]{3,2,1,0:T(8,128)(2,1)S(1)}, bf16[1,4,6,1024]{3,2,1,0:T(8,128)(2,1)S(1)}, u32[]{:S(2)}, u32[]{:S(2)}) collective-permute-start(bf16[1,4,6,1024]{3,2,1,0:T(8,128)(2,1)S(1)} %get-tuple-element.23), channel_id=1, source_target_pairs={{0,1},{2,3},{4,5},{6,7},{8,9},{10,11},{12,13},{14,15},{16,17},{18,... | collective-permute-start | bytes 147464 | tf_op jit(solution)/shard_map/ppermute | solution.py:17
  3.9 17.5 %collective-permute-start.1 = (bf16[1,4,6,1024]{3,2,1,0:T(8,128)(2,1)S(1)}, bf16[1,4,6,1024]{3,2,1,0:T(8,128)(2,1)S(1)}, u32[]{:S(2)}, u32[]{:S(2)}) collective-permute-start(bf16[1,4,6,1024]{3,2,1,0:T(8,128)(2,1)S(1)} %get-tuple-element.24), channel_id=1, source_target_pairs={{1,0},{3,2},{5,4},{7,6},{9,8},{11,10},{13,12},{15,14},{17,16},{19,... | collective-permute-start | bytes 147464 | tf_op jit(solution)/shard_map/ppermute | solution.py:20
  18.2 2.5 %copy-start.8 = (f32[2,4,7]{2,1,0:T(4,128)S(1)}, f32[2,4,7]{2,1,0:T(4,128)}, u32[]{:S(2)}) copy-start(f32[2,4,7]{2,1,0:T(4,128)} %param.4) | copy-start | bytes 676
  18.2 2.5 %copy-start.7 = (s32[8,8,8]{2,1,0:T(8,128)S(1)}, s32[8,8,8]{2,1,0:T(8,128)}, u32[]{:S(2)}) copy-start(s32[8,8,8]{2,1,0:T(8,128)} %param.5) | copy-start | bytes 6148
  18.2 3.2 %copy-start.1 = (bf16[1,4,256,1024]{3,2,1,0:T(8,128)(2,1)S(1)}, bf16[1,4,256,1024]{3,2,1,0:T(8,128)(2,1)}, u32[]{:S(2)}) copy-start(bf16[1,4,256,1024]{3,2,1,0:T(8,128)(2,1)} %param.3) | copy-start | bytes 6291460
  63.7 14.9 %all-to-all-start.2 = ((bf16[1,4,64,256]{3,1,0,2:T(4,128)(2,1)}), bf16[1,4,64,256]{3,1,0,2:T(4,128)(2,1)S(1)}, u32[]{:S(2)}, u32[]{:S(2)}) async-start(bf16[1,4,64,256]{3,1,0,2:T(4,128)(2,1)} %copy.28), calls=%async_computation.2 | async-start | bytes 262144 | tf_op jit(solution)/shard_map/all_to_all | solution.py:139
  78.6 22.7 %copy-start.4 = (bf16[1,4,64,256]{3,1,0,2:T(4,128)(2,1)}, bf16[1,4,64,256]{3,1,0,2:T(4,128)(2,1)S(1)}, u32[]{:S(2)}) copy-start(bf16[1,4,64,256]{3,1,0,2:T(4,128)(2,1)S(1)} %all-to-all-done.2) | copy-start | bytes 393220
  78.6 18.2 %all-to-all-start.1 = ((bf16[1,4,128,512]{3,1,0,2:T(4,128)(2,1)}), bf16[1,4,128,512]{3,1,0,2:T(4,128)(2,1)S(1)}, u32[]{:S(2)}, u32[]{:S(2)}) async-start(bf16[1,4,128,512]{3,1,0,2:T(4,128)(2,1)} %copy.23), calls=%async_computation.1 | async-start | bytes 1048576 | tf_op jit(solution)/shard_map/all_to_all | solution.py:136
  96.8 10.0 %copy-start.2 = (bf16[1,4,128,512]{3,1,0,2:T(4,128)(2,1)}, bf16[1,4,128,512]{3,1,0,2:T(4,128)(2,1)S(1)}, u32[]{:S(2)}) copy-start(bf16[1,4,128,512]{3,1,0,2:T(4,128)(2,1)S(1)} %all-to-all-done.1) | copy-start | bytes 1572868
  96.8 52.1 %all-to-all-start = ((bf16[8,1,4,32,1024]{4,3,2,1,0:T(8,128)(2,1)}), bf16[8,1,4,32,1024]{4,3,2,1,0:T(8,128)(2,1)S(1)}, u32[]{:S(2)}, u32[]{:S(2)}) async-start(bf16[8,1,4,32,1024]{4,3,2,1,0:T(8,128)(2,1)} %fusion.269), calls=%async_computation | async-start | bytes 4194304 | tf_op jit(solution)/shard_map/all_to_all | solution.py:128
  113.3 9.6 %copy-start.5 = (bf16[1,4,64,256]{3,1,0,2:T(4,128)(2,1)S(1)}, bf16[1,4,64,256]{3,1,0,2:T(4,128)(2,1)}, u32[]{:S(2)}) copy-start(bf16[1,4,64,256]{3,1,0,2:T(4,128)(2,1)} %copy-done.4) | copy-start | bytes 393220
  113.3 9.7 %copy-start.6 = (f32[8,8,256]{2,1,0:T(8,128)S(1)}, f32[8,8,256]{2,1,0:T(8,128)}, u32[]{:S(2)}) copy-start(f32[8,8,256]{2,1,0:T(8,128)} %fusion.295) | copy-start | bytes 196612
  115.3 8.7 %copy-start.3 = (bf16[1,4,128,512]{3,1,0,2:T(4,128)(2,1)S(1)}, bf16[1,4,128,512]{3,1,0,2:T(4,128)(2,1)}, u32[]{:S(2)}) copy-start(bf16[1,4,128,512]{3,1,0,2:T(4,128)(2,1)} %copy-done.2) | copy-start | bytes 1572868
  148.9 2.0 %copy-start = (f32[8,32,1024]{2,1,0:T(8,128)S(1)}, f32[8,32,1024]{2,1,0:T(8,128)}, u32[]{:S(2)}) copy-start(f32[8,32,1024]{2,1,0:T(8,128)} %get-tuple-element.29) | copy-start | bytes 3145732
